TPU v7x, 32 devices: a whole 2x2x4 slice. The times are simulated.
32 devices in a mesh: dp: 8 (over y, x, core), fsdp: 4 (over z).
Axes of the slice: x: 2, y: 2, z: 4, core: 2. Of those that a mesh axis runs over, the one named last changes fastest.
Arguments:
- query_cache: bfloat16 [384, 1024], P('dp', 'fsdp'), may hold values from -8 to 8
- region_cache: bfloat16 [384, 1024], P('dp', 'fsdp'), may hold values from -8 to 8
- positive: int32 [384], P('dp'), may hold values from 0 to 383, each once
- hidden_states: bfloat16 [4096, 4096], P(('dp', 'fsdp')), may hold values from -12 to 12
- segment_ids: int32 [8, 512], P('dp', 'fsdp'), may hold values from 0 to 47, never falling along the last dimension, each value on 1 to 21 neighbouring positions
- norm_gain: bfloat16 [4096], replicated, may hold values from 0.099609375 to 1.8984375
- proj_weight: bfloat16 [4096, 1024], P('fsdp'), may hold values from -1 to 1
Outputs:
- mean_loss: float32 [], replicated
- query_grad: float32 [384, 1024], P('dp', 'fsdp')
- region_grad: float32 [384, 1024], P('dp', 'fsdp')
- hidden_grad: bfloat16 [4096, 4096], P(('dp', 'fsdp'))
- gain_grad: float32 [4096], replicated
- proj_grad: float32 [4096, 1024], P('dp', 'fsdp')
Inputs may be any that keep to these rules, and one draw needn't show every extreme that they name: Each region is the positive of exactly one instruction. `segment_ids`: within a pair group the ids never fall, every instruction has at least one token, and one has exactly 21.
All inputs are finite; a program needn't handle non-finite values.
Results may differ from a plain program's by a relative error of at most 0.0088.
Values may be sent and summed in bfloat16 or wider, within the bound.
No kernel may reach another device: no remote copies, remote signals or barrier semaphores. Data moves between devices by JAX's collectives and lax.ppermute only.
A program may use at most 64 MiB of HBM per device.

v0:
```python
import jax
import jax.numpy as jnp
from jax import lax
from jax.sharding import PartitionSpec as P

E = 1024
EPS = 1e-05


def local(query_cache, region_cache, positive, hidden_states, segment_ids, norm_gain, proj_weight):
    row_count = query_cache.shape[0]
    data_count = lax.axis_size("dp")
    pair_count = row_count * data_count
    logit_scale = float(E) ** (-0.5)
    contract_last = (((1,), (1,)), ((), ()))
    contract_first = (((0,), (0,)), ((), ()))
    region_all, query_all = (
        lax.all_gather(region_cache, "dp", axis=0, tiled=True),
        lax.all_gather(query_cache, "dp", axis=0, tiled=True),
    )
    partial_value = lax.dot_general(
        query_cache, region_all, contract_last, preferred_element_type=jnp.float32
    )
    scores = lax.psum(partial_value, "fsdp") * logit_scale
    row_max = jnp.max(scores, axis=1, keepdims=True)
    log_total = row_max[:, 0] + jnp.log(jnp.sum(jnp.exp(scores - row_max), axis=1))
    columns = lax.broadcasted_iota(jnp.int32, (1, pair_count), 1)
    matched = columns == positive[:, None]
    target_score = jnp.sum(jnp.where(matched, scores, jnp.zeros_like(scores)), axis=1)
    loss_local = jnp.sum(log_total - target_score)
    grad_probs = (jnp.exp(scores - log_total[:, None]) - matched.astype(jnp.float32)).astype(
        jnp.bfloat16
    )
    query_grad = logit_scale * jnp.dot(grad_probs, region_all, preferred_element_type=jnp.float32)
    totals_all, targets_all = (
        lax.all_gather(log_total, "dp", axis=0, tiled=True),
        lax.all_gather(positive.astype(jnp.float32), "dp", axis=0, tiled=True),
    )
    partial_t = lax.dot_general(
        region_cache, query_all, contract_last, preferred_element_type=jnp.float32
    )
    scores_t = lax.psum(partial_t, "fsdp") * logit_scale
    own_rows = (
        lax.axis_index("dp") * row_count + lax.broadcasted_iota(jnp.int32, (row_count, 1), 0)
    ).astype(jnp.float32)
    matched_t = targets_all[None, :] == own_rows
    probs_t = (jnp.exp(scores_t - totals_all[None, :]) - matched_t.astype(jnp.float32)).astype(
        jnp.bfloat16
    )
    region_grad = logit_scale * jnp.dot(probs_t, query_all, preferred_element_type=jnp.float32)
    gain = norm_gain.astype(jnp.float32)
    states = hidden_states.astype(jnp.float32)
    inv_rms = lax.rsqrt(jnp.mean(states * states, axis=1, keepdims=True) + EPS)
    normed = (states * inv_rms * gain).astype(jnp.bfloat16)
    labels = lax.broadcasted_iota(jnp.int32, (row_count, 1), 0)
    member = segment_ids[0][None, :] == labels
    pooled_part = jnp.dot(member.astype(jnp.bfloat16), normed, preferred_element_type=jnp.float32)
    counts_part = jnp.sum(member.astype(jnp.float32), axis=1)
    pooled, counts = lax.psum((pooled_part, counts_part), "fsdp")
    mean_pooled = (pooled / counts[:, None]).astype(jnp.bfloat16)
    grad_low = query_grad.astype(jnp.bfloat16)
    grad_full = lax.all_gather(grad_low, "fsdp", axis=1, tiled=True)
    mean_part = lax.dot_general(
        grad_full, proj_weight, contract_last, preferred_element_type=jnp.float32
    )
    mean_grad = lax.all_gather(mean_part, "fsdp", axis=1, tiled=True)
    pool_grad = mean_grad / counts[:, None]
    normed_grad = lax.dot_general(
        member.astype(jnp.float32),
        pool_grad,
        contract_first,
        precision=lax.Precision.HIGHEST,
        preferred_element_type=jnp.float32,
    )
    gain_part = jnp.sum(normed_grad * states * inv_rms, axis=0)
    scaled = gain * normed_grad
    inner = jnp.mean(scaled * states, axis=1, keepdims=True)
    hidden_grad = (inv_rms * scaled - states * inv_rms**3 * inner).astype(jnp.bfloat16)
    proj_grad = lax.psum_scatter(
        lax.dot_general(mean_pooled, grad_low, contract_first, preferred_element_type=jnp.float32),
        "dp",
        scatter_dimension=0,
        tiled=True,
    )
    loss_total = lax.psum(loss_local, "dp")
    gain_grad = lax.psum(gain_part, ("dp", "fsdp"))
    mean_loss = loss_total / pair_count
    return (mean_loss, query_grad, region_grad, hidden_grad, gain_grad, proj_grad)


def solution(mesh):
    in_specs = (
        P("dp", "fsdp"),
        P("dp", "fsdp"),
        P("dp"),
        P(("dp", "fsdp"), None),
        P("dp", "fsdp"),
        P(),
        P("fsdp", None),
    )
    out_specs = (
        P(),
        P("dp", "fsdp"),
        P("dp", "fsdp"),
        P(("dp", "fsdp"), None),
        P(),
        P("dp", "fsdp"),
    )
    return jax.shard_map(local, mesh=mesh, in_specs=in_specs, out_specs=out_specs, check_vma=False)
```

profile of v0, /device:TPU:12, one launch (start us, length us, event | category | flops | bytes accessed | tf_op | source)
XLA Modules:
  0.0 194.4 jit_solution(16001850921238040908)
XLA Ops:
  7.2 0.0 all-reduce.6.cloned.1.call-start
  7.2 1.7 fusion
  8.9 0.6 multiply_multiply_fusion
  9.5 0.7 convert_element_type.53
  10.2 9.2 %all_gather.19 = bf16[384,256]{1,0:T(8,128)(2,1)S(1)} all-gather(bf16[48,256]{1,0:T(8,128)(2,1)} %param.7), channel_id=1, replica_groups=mesh['dp'=8,'fsdp'=4] {'dp'}, dimensions={0}, use_global_device_ids=true | all-gather | bytes 221184 | tf_op jit(solution)/shard_map/all_gather | solution.py:19
  19.5 8.5 %all_gather.18 = bf16[384,256]{1,0:T(8,128)(2,1)S(1)} all-gather(bf16[48,256]{1,0:T(8,128)(2,1)} %param.8), channel_id=1, replica_groups=mesh['dp'=8,'fsdp'=4] {'dp'}, dimensions={0}, use_global_device_ids=true | all-gather | bytes 221184 | tf_op jit(solution)/shard_map/all_gather | solution.py:18
  27.9 1.6 fusion.32
  29.5 1.6 fusion.31
  31.1 1.4 fusion.9
  32.4 0.0 reduce-scatter.2.cloned.1.call-start
  32.5 1.2 dynamic-slice
  34.4 1.3 convert_reduce_fusion
  35.7 9.7 %psum.45 = f32[48]{0:T(128)} all-reduce(f32[48]{0:T(128)} %convert_reduce_fusion), channel_id=1, replica_groups=mesh['dp'=8,'fsdp'=4] {'fsdp'}, use_global_device_ids=true, to_apply=%region_9.10 | all-reduce | flops 48 | bytes 384 | tf_op jit(solution)/shard_map/psum | solution.py:59
  45.4 37.4 %all-reduce.6.cloned.1.call-done = (f32[48,384]{1,0:T(8,128)}, f32[48,384]{1,0:T(8,128)}, f32[48,4096]{1,0:T(8,128)}) async-done(((f32[48,384]{1,0:T(8,128)}, f32[48,384]{1,0:T(8,128)}, f32[48,4096]{1,0:T(8,128)}), (f32[48,384]{1,0:T(8,128)}, f32[48,384]{1,0:T(8,128)}, f32[48,4096]{1,0:T(8,128)})) %all-reduce.6.cloned.1.call-update) | async-done | bytes 933904 | tf_op jit(solution)/shard_map/psum | solution.py:24
  82.8 1.0 multiply_reduce_fusion
  83.8 1.6 select_reduce_fusion
  85.4 0.1 fusion.29
  85.5 1.7 fusion.30
  87.2 0.6 copy-done.2
  87.9 3.9 %fusion.15 = f32[4096,256]{1,0:T(8,128)} fusion(bf16[48,256]{1,0:T(8,128)(2,1)S(1)} %get-tuple-element.20, f32[48,4096]{1,0:T(8,128)} %get-tuple-element.15, f32[48]{0:T(128)} %psum.45), kind=kOutput, calls=%fused_computation.22 | convolution fusion | flops 101056512 | bytes 5005504 | tf_op jit(solution)/shard_map/dot_general | solution.py:80
  91.8 0.0 reduce-scatter.2.cloned.1.call-update
  91.9 0.5 copy-done.7
  92.4 0.1 convert_dynamic-update-slice_fusion
  92.5 0.6 subtract_reduce_fusion
  93.1 13.3 %all-reduce.2 = (f32[]{:T(128)}, f32[384]{0:T(512)S(1)}, f32[384]{0:T(512)S(1)}) all-reduce(f32[]{:T(128)} %subtract_reduce_fusion, f32[384]{0:T(512)S(1)} %convert_dynamic-update-slice_fusion, f32[384]{0:T(512)S(1)} %copy-done.6), channel_id=1, replica_groups=mesh['dp'=8,'fsdp'=4] {'dp'}, use_global_device_ids=true, to_apply=%region_5.6 | all-reduce | flops 769 | bytes 6152 | tf_op jit(solution)/shard_map/psum | solution.py:85
  107.1 12.2 %all_gather.22 = bf16[48,1024]{1,0:T(8,128)(2,1)S(1)} all-gather(bf16[48,256]{1,0:T(8,128)(2,1)S(1)} %copy-done.3), channel_id=1, replica_groups=mesh['dp'=8,'fsdp'=4] {'fsdp'}, dimensions={1}, use_global_device_ids=true | all-gather | bytes 122880 | tf_op jit(solution)/shard_map/all_gather | solution.py:62
  119.3 0.7 fusion.33
  120.0 17.5 %all_gather.23 = f32[48,4096]{1,0:T(8,128)S(1)} all-gather(f32[48,1024]{1,0:T(8,128)S(1)} %fusion.33), channel_id=1, replica_groups=mesh['dp'=8,'fsdp'=4] {'fsdp'}, dimensions={1}, use_global_device_ids=true | all-gather | bytes 983040 | tf_op jit(solution)/shard_map/all_gather | solution.py:66
  137.6 2.8 %fusion.6 = (f32[4096]{0:T(1024)S(1)}, f32[128]{0:T(128)S(1)}, f32[128,4096]{1,0:T(8,128)}) fusion(bf16[128,4096]{1,0:T(8,128)(2,1)S(1)} %copy-done.1, f32[128]{0:T(128)S(1)} %copy-done.12, f32[4096]{0:T(1024)S(1)} %convert_element_type.53, f32[48,4096]{1,0:T(8,128)S(1)} %all_gather.23, f32[48]{0:T(128)S(1)} %copy-done.13, s32[128]{0:T(128)S(1)} %bitcast.13), kind=kOutput, calls=%fused_computation.11 | convolution fusion | flops 305858432 | bytes 3966656 | tf_op jit(solution)/shard_map/dot_general | solution.py:68
  140.4 42.0 %psum.46 = f32[4096]{0:T(1024)} all-reduce(f32[4096]{0:T(1024)S(1)} %get-tuple-element.6), channel_id=1, replica_groups=mesh['dp'=8,'fsdp'=4] {'dp','fsdp'}, use_global_device_ids=true, to_apply=%region_12.13 | all-reduce | flops 4096 | bytes 32768 | tf_op jit(solution)/shard_map/psum | solution.py:86
  182.5 0.8 convolution_multiply_fusion
  183.3 3.2 %fusion.3 = bf16[128,4096]{1,0:T(8,128)(2,1)} fusion(bf16[128,4096]{1,0:T(8,128)(2,1)S(1)} %copy-done.1, f32[128,4096]{1,0:T(8,128)} %get-tuple-element.22, f32[128]{0:T(128)S(1)} %broadcast_multiply_fusion, f32[128]{0:T(128)S(1)} %copy-done.10, f32[4096]{0:T(1024)S(1)} %convert_element_type.53, f32[128]{0:T(128)S(1)} %copy-done.12), kind=kLoop, calls=%fused_computation.8 | loop fusion | flops 3670016 | bytes 4212224 | tf_op jit(solution)/shard_map/convert_element_type | solution.py:78
  (38 shorter events, 0.1 us)
Async XLA Ops:
  7.2 112.1 %copy-start = (bf16[1024,1024]{1,0:T(8,128)(2,1)S(1)}, bf16[1024,1024]{1,0:T(8,128)(2,1)}, u32[]{:S(2)}) copy-start(bf16[1024,1024]{1,0:T(8,128)(2,1)} %param.13) | copy-start | bytes 6291460
  7.2 23.9 %copy-start.1 = (bf16[128,4096]{1,0:T(8,128)(2,1)S(1)}, bf16[128,4096]{1,0:T(8,128)(2,1)}, u32[]{:S(2)}) copy-start(bf16[128,4096]{1,0:T(8,128)(2,1)} %param.10) | copy-start | bytes 3145732
  7.2 75.6 %all-reduce.6.cloned.1.call-start = ((), (), s32[]{:S(2)}) async-start(), calls=%async_computation.2 | async-start | bytes 1867776 | tf_op jit(solution)/shard_map/psum | solution.py:24
  7.2 23.8 %copy-start.15 = (s32[1,128]{1,0:T(1,128)S(1)}, s32[1,128]{1,0:T(1,128)}, u32[]{:S(2)}) copy-start(s32[1,128]{1,0:T(1,128)} %param.11) | copy-start | bytes 1540
  9.5 21.5 %copy-start.11 = (f32[128]{0:T(128)}, f32[128]{0:T(128)S(1)}, u32[]{:S(2)}) copy-start(f32[128]{0:T(128)S(1)} %get-tuple-element.19) | copy-start | bytes 1540
  32.4 154.0 %reduce-scatter.2.cloned.1.call-start = ((), (), s32[]{:S(2)}) async-start(), calls=%async_computation.1 | async-start | bytes 4718592 | tf_op jit(solution)/shard_map/reduce_scatter | solution.py:79
  85.5 1.7 copy-start.5
  85.5 1.7 copy-start.8
  87.2 0.6 copy-start.2
  91.7 0.7 copy-start.7
  91.7 0.7 copy-start.9
  91.8 0.7 copy-start.14
  91.8 1.3 copy-start.6
  91.8 15.3 %copy-start.3 = (bf16[48,256]{1,0:T(8,128)(2,1)S(1)}, bf16[48,256]{1,0:T(8,128)(2,1)}, u32[]{:S(2)}) copy-start(bf16[48,256]{1,0:T(8,128)(2,1)} %copy-done.2) | copy-start | bytes 73732
  91.8 45.8 %copy-start.12 = (f32[128]{0:T(128)S(1)}, f32[128]{0:T(128)}, u32[]{:S(2)}) copy-start(f32[128]{0:T(128)} %copy-done.11) | copy-start | bytes 1540
  91.8 45.8 %copy-start.13 = (f32[48]{0:T(128)S(1)}, f32[48]{0:T(128)}, u32[]{:S(2)}) copy-start(f32[48]{0:T(128)} %psum.45) | copy-start | bytes 580
  91.8 45.8 %copy-start.16 = (s32[1,128]{1,0:T(1,128)S(1)}, s32[1,128]{1,0:T(1,128)}, u32[]{:S(2)}) copy-start(s32[1,128]{1,0:T(1,128)} %param.11) | copy-start | bytes 1540
  137.6 44.9 %copy-start.4 = (f32[48,384]{1,0:T(8,128)S(1)}, f32[48,384]{1,0:T(8,128)}, u32[]{:S(2)}) copy-start(f32[48,384]{1,0:T(8,128)} %get-tuple-element.14) | copy-start | bytes 221188
  137.6 45.7 %copy-start.10 = (f32[128]{0:T(128)S(1)}, f32[128]{0:T(128)}, u32[]{:S(2)}) copy-start(f32[128]{0:T(128)} %get-tuple-element.18) | copy-start | bytes 1540
Sparse Core Ops, SparseCore 0:
  32.6 50.2 all-reduce.5
  91.9 50.7 reduce-scatter.1
where the time goes:
time: 195 us; the launch traced here: 194 us
  blocking collectives  113 us (58%)
  waiting for transfers between devices  37.4 us (19%)
  between operations  16.6 us (9%)
  matrix products  14.5 us (7%)
  other arithmetic  10.8 us (6%)
  local copies, waits for them, and re-layouts  2.47 us (1%)
    psum x1, blocking collectives, local(): gain_grad = lax.psum(gain_part, ('dp', 'fsdp'))  42 us
    psum x1, waiting for transfers between devices, local(): scores = lax.psum(partial_value, 'fsdp') * logit_scale  37.4 us
    all_gather x1, blocking collectives, local(): mean_grad = lax.all_gather(mean_part, 'fsdp', axis=1, tiled=True)  17.5 us
    psum x1, blocking collectives, local(): loss_total = lax.psum(loss_local, 'dp')  13.3 us
    all_gather x1, blocking collectives, local(): grad_full = lax.all_gather(grad_low, 'fsdp', axis=1, tiled=True)  12.2 us
    psum x1, blocking collectives, local(): pooled, counts = lax.psum((pooled_part, counts_part), 'fsdp')  9.73 us
    all_gather x1, blocking collectives, local(): lax.all_gather(query_cache, 'dp', axis=0, tiled=True)  9.23 us
    all_gather x1, blocking collectives, local(): lax.all_gather(region_cache, 'dp', axis=0, tiled=True)  8.47 us
  transfers between devices with their start and end apart: 2, of which 1 were waited for; matrix products, arithmetic and copies ran while one was open for 6% of the time, Pallas kernels for 0%

commit v1 on v0

--- a/solution.py
+++ b/solution.py
@@ -83,7 +83,7 @@
         tiled=True,
     )
     loss_total = lax.psum(loss_local, "dp")
-    gain_grad = lax.psum(gain_part, ("dp", "fsdp"))
+    gain_grad = lax.psum(lax.psum(gain_part, "fsdp"), "dp")
     mean_loss = loss_total / pair_count
     return (mean_loss, query_grad, region_grad, hidden_grad, gain_grad, proj_grad)
 

time: 195 us -> 184 us (0.944)
  the two profiles are of different devices: /device:TPU:12 before, /device:TPU:0 now
where the time goes in v1:
time: 184 us; the launch traced here: 183 us
  blocking collectives  105 us (57%)
  waiting for transfers between devices  33.7 us (18%)
  between operations  16.6 us (9%)
  matrix products  14.5 us (8%)
  other arithmetic  10.8 us (6%)
  local copies, waits for them, and re-layouts  2.5 us (1%)
    psum x1, waiting for transfers between devices, local(): scores = lax.psum(partial_value, 'fsdp') * logit_scale  33.7 us
    psum x1, blocking collectives, local(): loss_total = lax.psum(loss_local, 'dp')  23.5 us
    psum x1, blocking collectives, local(): gain_grad = lax.psum(lax.psum(gain_part, 'fsdp'), 'dp')  17.5 us
    all_gather x1, blocking collectives, local(): mean_grad = lax.all_gather(mean_part, 'fsdp', axis=1, tiled=True)  17.1 us
    all_gather x1, blocking collectives, local(): grad_full = lax.all_gather(grad_low, 'fsdp', axis=1, tiled=True)  13.5 us
    psum x1, blocking collectives, local(): pooled, counts = lax.psum((pooled_part, counts_part), 'fsdp')  13 us
    all_gather x1, blocking collectives, local(): lax.all_gather(query_cache, 'dp', axis=0, tiled=True)  10.9 us
    all_gather x1, blocking collectives, local(): lax.all_gather(region_cache, 'dp', axis=0, tiled=True)  9.04 us
  transfers between devices with their start and end apart: 2, of which 1 were waited for; matrix products, arithmetic and copies ran while one was open for 6% of the time, Pallas kernels for 0%

profile of v1, /device:TPU:0, one launch (start us, length us, event | category | flops | bytes accessed | tf_op | source)
XLA Modules:
  0.0 182.7 jit_solution(4440469757987572090)
XLA Ops:
  7.2 0.0 all-reduce.6.cloned.1.call-start
  7.2 1.7 fusion
  8.9 0.6 multiply_multiply_fusion
  9.5 0.7 convert_element_type.53
  10.2 10.9 %all_gather.19 = bf16[384,256]{1,0:T(8,128)(2,1)S(1)} all-gather(bf16[48,256]{1,0:T(8,128)(2,1)} %param.7), channel_id=1, replica_groups=mesh['dp'=8,'fsdp'=4] {'dp'}, dimensions={0}, use_global_device_ids=true | all-gather | bytes 221184 | tf_op jit(solution)/shard_map/all_gather | solution.py:19
  21.1 9.0 %all_gather.18 = bf16[384,256]{1,0:T(8,128)(2,1)S(1)} all-gather(bf16[48,256]{1,0:T(8,128)(2,1)} %param.8), channel_id=1, replica_groups=mesh['dp'=8,'fsdp'=4] {'dp'}, dimensions={0}, use_global_device_ids=true | all-gather | bytes 221184 | tf_op jit(solution)/shard_map/all_gather | solution.py:18
  30.2 1.6 fusion.32
  31.7 1.6 fusion.31
  33.3 1.4 fusion.9
  34.7 0.0 all-reduce.6.cloned.1.call-update
  34.7 0.0 reduce-scatter.2.cloned.1.call-start
  34.7 1.2 dynamic-slice
  36.6 1.3 convert_reduce_fusion
  37.9 13.0 %psum.52 = f32[48]{0:T(128)} all-reduce(f32[48]{0:T(128)} %convert_reduce_fusion), channel_id=1, replica_groups=mesh['dp'=8,'fsdp'=4] {'fsdp'}, use_global_device_ids=true, to_apply=%region_9.10 | all-reduce | flops 48 | bytes 384 | tf_op jit(solution)/shard_map/psum | solution.py:59
  51.0 33.7 %all-reduce.6.cloned.1.call-done = (f32[48,384]{1,0:T(8,128)}, f32[48,384]{1,0:T(8,128)}, f32[48,4096]{1,0:T(8,128)}) async-done(((f32[48,384]{1,0:T(8,128)}, f32[48,384]{1,0:T(8,128)}, f32[48,4096]{1,0:T(8,128)}), (f32[48,384]{1,0:T(8,128)}, f32[48,384]{1,0:T(8,128)}, f32[48,4096]{1,0:T(8,128)})) %all-reduce.6.cloned.1.call-update) | async-done | bytes 933904 | tf_op jit(solution)/shard_map/psum | solution.py:24
  84.6 1.0 multiply_reduce_fusion
  85.6 1.6 select_reduce_fusion
  87.2 0.1 fusion.29
  87.3 1.7 fusion.30
  89.1 0.6 copy-done.2
  89.7 3.9 %fusion.15 = f32[4096,256]{1,0:T(8,128)} fusion(bf16[48,256]{1,0:T(8,128)(2,1)S(1)} %get-tuple-element.21, f32[48,4096]{1,0:T(8,128)} %get-tuple-element.16, f32[48]{0:T(128)} %psum.52), kind=kOutput, calls=%fused_computation.22 | convolution fusion | flops 101056512 | bytes 5005504 | tf_op jit(solution)/shard_map/dot_general | solution.py:80
  93.6 0.6 copy-done.7
  94.2 0.1 convert_dynamic-update-slice_fusion
  94.3 13.5 %all_gather.22 = bf16[48,1024]{1,0:T(8,128)(2,1)S(1)} all-gather(bf16[48,256]{1,0:T(8,128)(2,1)S(1)} %copy-done.3), channel_id=1, replica_groups=mesh['dp'=8,'fsdp'=4] {'fsdp'}, dimensions={1}, use_global_device_ids=true | all-gather | bytes 122880 | tf_op jit(solution)/shard_map/all_gather | solution.py:62
  107.8 0.7 fusion.33
  108.5 17.1 %all_gather.23 = f32[48,4096]{1,0:T(8,128)S(1)} all-gather(f32[48,1024]{1,0:T(8,128)S(1)} %fusion.33), channel_id=1, replica_groups=mesh['dp'=8,'fsdp'=4] {'fsdp'}, dimensions={1}, use_global_device_ids=true | all-gather | bytes 983040 | tf_op jit(solution)/shard_map/all_gather | solution.py:66
  125.7 2.8 %fusion.6 = (f32[4096]{0:T(1024)S(1)}, f32[128]{0:T(128)S(1)}, f32[128,4096]{1,0:T(8,128)}) fusion(bf16[128,4096]{1,0:T(8,128)(2,1)S(1)} %copy-done.1, f32[128]{0:T(128)S(1)} %copy-done.12, f32[4096]{0:T(1024)S(1)} %convert_element_type.53, f32[48,4096]{1,0:T(8,128)S(1)} %all_gather.23, f32[48]{0:T(128)S(1)} %copy-done.13, s32[128]{0:T(128)S(1)} %bitcast.13), kind=kOutput, calls=%fused_computation.11 | convolution fusion | flops 305858432 | bytes 3966656 | tf_op jit(solution)/shard_map/dot_general | solution.py:68
  128.5 17.5 %psum.53 = f32[4096]{0:T(1024)S(1)} all-reduce(f32[4096]{0:T(1024)S(1)} %get-tuple-element.6), channel_id=1, replica_groups=mesh['dp'=8,'fsdp'=4] {'fsdp'}, use_global_device_ids=true, to_apply=%region_12.13 | all-reduce | flops 4096 | bytes 32768 | tf_op jit(solution)/shard_map/psum | solution.py:86
  146.0 0.6 subtract_reduce_fusion
  146.6 23.5 %all-reduce.2 = (f32[]{:T(128)}, f32[384]{0:T(512)S(1)}, f32[384]{0:T(512)S(1)}, f32[4096]{0:T(1024)}) all-reduce(f32[]{:T(128)} %subtract_reduce_fusion, f32[384]{0:T(512)S(1)} %convert_dynamic-update-slice_fusion, f32[384]{0:T(512)S(1)} %copy-done.6, f32[4096]{0:T(1024)S(1)} %psum.53), channel_id=1, replica_groups=mesh['dp'=8,'fsdp'=4] {'dp'}, use_global_device_ids=true, to_apply=%region_5.6 | all-reduce | flops 4865 | bytes 38920 | tf_op jit(solution)/shard_map/psum | solution.py:85
  170.8 0.8 convolution_multiply_fusion
  171.6 3.2 %fusion.3 = bf16[128,4096]{1,0:T(8,128)(2,1)} fusion(bf16[128,4096]{1,0:T(8,128)(2,1)S(1)} %copy-done.1, f32[128,4096]{1,0:T(8,128)} %get-tuple-element.23, f32[128]{0:T(128)S(1)} %broadcast_multiply_fusion, f32[128]{0:T(128)S(1)} %copy-done.10, f32[4096]{0:T(1024)S(1)} %convert_element_type.53, f32[128]{0:T(128)S(1)} %copy-done.12), kind=kLoop, calls=%fused_computation.8 | loop fusion | flops 3670016 | bytes 4212224 | tf_op jit(solution)/shard_map/convert_element_type | solution.py:78
  (38 shorter events, 0.1 us)
Async XLA Ops:
  7.2 100.6 %copy-start = (bf16[1024,1024]{1,0:T(8,128)(2,1)S(1)}, bf16[1024,1024]{1,0:T(8,128)(2,1)}, u32[]{:S(2)}) copy-start(bf16[1024,1024]{1,0:T(8,128)(2,1)} %param.13) | copy-start | bytes 6291460
  7.2 26.1 %copy-start.1 = (bf16[128,4096]{1,0:T(8,128)(2,1)S(1)}, bf16[128,4096]{1,0:T(8,128)(2,1)}, u32[]{:S(2)}) copy-start(bf16[128,4096]{1,0:T(8,128)(2,1)} %param.10) | copy-start | bytes 3145732
  7.2 77.4 %all-reduce.6.cloned.1.call-start = ((), (), s32[]{:S(2)}) async-start(), calls=%async_computation.2 | async-start | bytes 1867776 | tf_op jit(solution)/shard_map/psum | solution.py:24
  7.2 26.1 %copy-start.15 = (s32[1,128]{1,0:T(1,128)S(1)}, s32[1,128]{1,0:T(1,128)}, u32[]{:S(2)}) copy-start(s32[1,128]{1,0:T(1,128)} %param.11) | copy-start | bytes 1540
  9.5 23.8 %copy-start.11 = (f32[128]{0:T(128)}, f32[128]{0:T(128)S(1)}, u32[]{:S(2)}) copy-start(f32[128]{0:T(128)S(1)} %get-tuple-element.20) | copy-start | bytes 1540
  34.7 140.1 %reduce-scatter.2.cloned.1.call-start = ((), (), s32[]{:S(2)}) async-start(), calls=%async_computation.1 | async-start | bytes 4718592 | tf_op jit(solution)/shard_map/reduce_scatter | solution.py:79
  87.3 1.7 copy-start.5
  87.3 1.7 copy-start.8
  89.0 0.6 copy-start.2
  93.6 0.7 copy-start.7
  93.6 0.8 copy-start.3
  93.6 32.0 %copy-start.12 = (f32[128]{0:T(128)S(1)}, f32[128]{0:T(128)}, u32[]{:S(2)}) copy-start(f32[128]{0:T(128)} %copy-done.11) | copy-start | bytes 1540
  93.6 32.0 %copy-start.13 = (f32[48]{0:T(128)S(1)}, f32[48]{0:T(128)}, u32[]{:S(2)}) copy-start(f32[48]{0:T(128)} %psum.52) | copy-start | bytes 580
  93.6 32.0 %copy-start.16 = (s32[1,128]{1,0:T(1,128)S(1)}, s32[1,128]{1,0:T(1,128)}, u32[]{:S(2)}) copy-start(s32[1,128]{1,0:T(1,128)} %param.11) | copy-start | bytes 1540
  125.6 20.4 %copy-start.9 = (f32[48]{0:T(128)S(1)}, f32[48]{0:T(128)}, u32[]{:S(2)}) copy-start(f32[48]{0:T(128)} %copy-done.8) | copy-start | bytes 580
  125.6 20.3 %copy-start.14 = (f32[48]{0:T(128)S(1)}, f32[48]{0:T(128)}, u32[]{:S(2)}) copy-start(f32[48]{0:T(128)} %get-tuple-element.8) | copy-start | bytes 580
  125.7 20.9 %copy-start.6 = (f32[384]{0:T(512)S(1)}, f32[384]{0:T(512)}, u32[]{:S(2)}) copy-start(f32[384]{0:T(512)} %copy-done.5) | copy-start | bytes 4612
  125.7 45.1 %copy-start.4 = (f32[48,384]{1,0:T(8,128)S(1)}, f32[48,384]{1,0:T(8,128)}, u32[]{:S(2)}) copy-start(f32[48,384]{1,0:T(8,128)} %get-tuple-element.15) | copy-start | bytes 221188
  125.7 45.9 %copy-start.10 = (f32[128]{0:T(128)S(1)}, f32[128]{0:T(128)}, u32[]{:S(2)}) copy-start(f32[128]{0:T(128)} %get-tuple-element.19) | copy-start | bytes 1540
Sparse Core Ops, SparseCore 0:
  34.8 49.7 all-reduce.5
  93.7 50.6 reduce-scatter.1
